TPU v7x, 512 devices: a whole 4x8x8 slice. The times are simulated.
512 devices in a mesh: member: 16 (over x_lo, y), dp: 32 (over z, x_hi, core).
Axes of the slice: x: 4 (x_hi: 2, x_lo: 2; x = x_hi * 2 + x_lo), y: 8, z: 8, core: 2. Of those that a mesh axis runs over, the one named last changes fastest.
Arguments:
- inputs: bfloat16 [8192, 64], P('dp'), may hold values from -6 to 6
- observed: float32 [64, 8192], P('member', 'dp'), may hold values from -6 to 6
- noise: bfloat16 [2, 32, 64, 8192], P(None, None, 'member', 'dp'), may hold values from -4 to 4
- w_in: float32 [32, 64, 4096], P('member', None, 'dp'), may hold values from -0.75 to 0.75
- b_in: float32 [32, 4096], P('member', 'dp'), may hold values from -3 to 3
- w_out: float32 [32, 64, 4096], P('member', None, 'dp'), may hold values from -0.09375 to 0.09375
- b_out: float32 [32, 64], P('member'), may hold values from -3 to 3
Outputs:
- new_w_in: float32 [32, 64, 4096], P('member', None, 'dp')
- new_b_in: float32 [32, 4096], P('member', 'dp')
- new_w_out: float32 [32, 64, 4096], P('member', None, 'dp')
- new_b_out: float32 [32, 64], P('member')
All inputs are finite; a program needn't handle non-finite values.
Results may differ from a plain program's by a relative error of at most 0.00056.
Values may be sent and summed in bfloat16 or wider, within the bound.
No kernel may reach another device: no remote copies, remote signals or barrier semaphores. Data moves between devices by JAX's collectives and lax.ppermute only.
A program may use at most 64 MiB of HBM per device.

v0:
```python
import jax
import jax.numpy as jnp
from jax import lax
from jax.sharding import PartitionSpec as P

UPDATES = 2
ridge_level = 0.5


def solve_gain(gram, cross):
    eye = jnp.eye(gram.shape[0], dtype=gram.dtype)
    factor = jnp.linalg.cholesky(gram + ridge_level * eye)
    middle = lax.linalg.triangular_solve(factor, cross, left_side=True, lower=True)
    return lax.linalg.triangular_solve(factor, middle, left_side=True, lower=True, transpose_a=True)


def pack(w_in, b_in, w_out, b_out):
    n = w_in.shape[0]
    return jnp.concatenate(
        [w_in.reshape(n, -1), w_out.reshape(n, -1), b_in.reshape(n, -1), b_out.reshape(n, -1)],
        axis=1,
    )


def unpack(flat, f_in, hid, outs):
    n = flat.shape[0]
    a = f_in * hid
    b = a + outs * hid
    c = b + hid
    return (
        flat[:, :a].reshape(n, f_in, hid),
        flat[:, b:c].reshape(n, hid),
        flat[:, a:b].reshape(n, outs, hid),
        flat[:, c:].reshape(n, outs),
    )


def predict(inputs, own_flat, b_out, f_in, hid, outs):
    n = own_flat.shape[0]
    a = f_in * hid
    b = a + outs * hid
    rounded = own_flat[:, : b + hid].astype(jnp.bfloat16)
    gathered = lax.all_gather(rounded, "dp", axis=0, tiled=False)
    d = gathered.shape[0]
    w_in = gathered[:, :, :a].reshape(d, n, f_in, hid)
    w_out = gathered[:, :, a:b].reshape(d, n, outs, hid)
    b_in = gathered[:, :, b : b + hid]
    pre = jnp.einsum("sf,dnfh->nsdh", inputs, w_in, preferred_element_type=jnp.float32)
    pre = pre + jnp.transpose(b_in, (1, 0, 2)).astype(jnp.float32)[:, None, :, :]
    hidden = jnp.tanh(pre).astype(jnp.bfloat16)
    pred = jnp.einsum("dnoh,nsdh->nos", w_out, hidden, preferred_element_type=jnp.float32)
    return pred + b_out[:, :, None]


def on_device(inputs, observed, noise, w_in, b_in, w_out, b_out):
    per_device = w_in.shape[0]
    f_in, hid = (w_in.shape[1], w_in.shape[2])
    outs = w_out.shape[1]
    count = observed.shape[0] * lax.axis_size("member") * observed.shape[1] * lax.axis_size("dp")
    first = lax.axis_index("member") * per_device
    own = pack(w_in, b_in, w_out, b_out)
    whole = lax.all_gather(own, "member", axis=0, tiled=True)
    for update in range(UPDATES):
        own_b_out = own[:, -outs:]
        predicted = predict(inputs, own, own_b_out, f_in, hid, outs)
        collected = lax.all_to_all(predicted, "member", split_axis=1, concat_axis=0, tiled=True)
        mean_pred = jnp.mean(collected, axis=0)
        anomaly = (collected - mean_pred[None]).reshape(collected.shape[0], -1)
        misfit = (observed[None] + noise[update].astype(jnp.float32) - collected).reshape(
            collected.shape[0], -1
        )
        gram_part = lax.dot_general(
            anomaly, anomaly, (((1,), (1,)), ((), ())), precision=lax.Precision.HIGHEST
        )
        cross_part = lax.dot_general(
            anomaly, misfit, (((1,), (1,)), ((), ())), precision=lax.Precision.HIGHEST
        )
        gram, cross = lax.psum((gram_part, cross_part), ("member", "dp"))
        gain = solve_gain(gram / count, cross / count)
        if update + 1 < UPDATES:
            moved = lax.dot_general(
                gain, whole, (((0,), (0,)), ((), ())), precision=lax.Precision.HIGHEST
            )
            whole = whole + moved
            own = lax.dynamic_slice_in_dim(whole, first, per_device, 0)
        else:
            columns = lax.dynamic_slice_in_dim(gain, first, per_device, 1)
            moved = lax.dot_general(
                columns, whole, (((0,), (0,)), ((), ())), precision=lax.Precision.HIGHEST
            )
            own = own + moved
    return unpack(own, f_in, hid, outs)


def solution(mesh):
    placed = (
        P("dp", None),
        P("member", "dp"),
        P(None, None, "member", "dp"),
        P("member", None, "dp"),
        P("member", "dp"),
        P("member", None, "dp"),
        P("member", None),
    )
    return jax.shard_map(
        on_device,
        mesh=mesh,
        in_specs=placed,
        out_specs=(
            P("member", None, "dp"),
            P("member", "dp"),
            P("member", None, "dp"),
            P("member", None),
        ),
        check_vma=False,
    )
```

profile of v0, /device:TPU:1, one launch (start us, length us, event | category | flops | bytes accessed | tf_op | source)
XLA Modules:
  0.0 511.3 jit_solution(14198276268625181387)
XLA Ops:
  7.2 0.7 convert_bitcast_fusion.2
  7.9 0.8 convert.20
  8.8 0.8 convert.19
  10.4 1.0 copy_bitcast_fusion.2
  11.4 1.4 maximum_bitcast_fusion
  12.8 90.6 %all-gather.7.cloned.1.call-done = bf16[32,2,16512]{2,1,0:T(2,128)(2,1)} async-done(((bf16[1,2,16512]{2,1,0:T(2,128)(2,1)}), bf16[32,2,16512]{2,1,0:T(2,128)(2,1)}) %all-gather.7.cloned.1.call-update) | async-done | bytes 2113552 | tf_op jit(solution)/shard_map/all_gather | solution.py:43
  103.4 0.7 convert_bitcast_fusion.1
  104.1 2.9 fusion.60
  107.1 0.8 reshape.148
  107.9 0.8 reshape.147
  108.8 2.5 fusion.20
  111.3 0.7 copy.43
  112.1 6.6 %all-to-all-start = ((f32[2,64,256]{2,0,1:T(2,128)}), f32[2,64,256]{2,0,1:T(2,128)S(1)}, u32[]{:S(2)}, u32[]{:S(2)}) async-start(f32[2,64,256]{2,0,1:T(2,128)} %copy.43), calls=%async_computation | async-start | bytes 262144 | tf_op jit(solution)/shard_map/all_to_all | solution.py:66
  118.8 47.6 %all-gather.9.cloned.1.call-done = f32[16,2,16576]{2,1,0:T(2,128)} async-done(((f32[1,2,16576]{2,1,0:T(2,128)}), f32[16,2,16576]{2,1,0:T(2,128)}) %all-gather.9.cloned.1.call-update) | async-done | bytes 2121744 | tf_op jit(solution)/shard_map/all_gather | solution.py:62
  166.4 3.7 reshape.128
  170.7 107.1 %all-reduce.1 = (f32[32,32]{0,1:T(8,128)S(1)}, f32[32,32]{0,1:T(8,128)S(1)}) all-reduce(f32[32,32]{0,1:T(8,128)S(1)} %convolution_bitcast_fusion.3, f32[32,32]{0,1:T(8,128)S(1)} %convolution_bitcast_fusion.2), channel_id=1, replica_groups=mesh['member'=16,'dp'=32] {'member','dp'}, use_global_device_ids=true, to_apply=%region_1.0 | all-reduce | flops 2048 | bytes 16384 | tf_op jit(solution)/shard_map/psum | solution.py:78
  277.9 2.9 cholesky.44
  282.1 2.4 custom-call.11
  285.0 4.2 convolution_add_fusion
  289.1 0.7 fusion.35
  289.9 80.4 %all-gather.11.cloned.1.call-done = bf16[32,2,16512]{2,1,0:T(2,128)(2,1)} async-done(((bf16[1,2,16512]{2,1,0:T(2,128)(2,1)}), bf16[32,2,16512]{2,1,0:T(2,128)(2,1)}) %all-gather.11.cloned.1.call-update) | async-done | bytes 2113552 | tf_op jit(solution)/shard_map/all_gather | solution.py:43
  370.3 4.0 fusion.59
  374.4 2.6 reshape.116
  377.0 0.7 convert_bitcast_fusion
  377.8 1.6 reshape.149
  379.4 3.2 fusion.1
  382.6 0.8 fusion.17
  383.6 13.8 %all_to_all.30 = f32[2,64,256]{2,0,1:T(2,128)S(1)} all-to-all(f32[2,64,256]{2,0,1:T(2,128)S(1)} %copy.55), channel_id=1, replica_groups=mesh['member'=16,'dp'=32] {'member'}, dimensions={1} | all-to-all | bytes 262144 | tf_op jit(solution)/shard_map/all_to_all | solution.py:66
  398.0 96.0 %all-reduce = (f32[32,32]{0,1:T(8,128)S(1)}, f32[32,32]{0,1:T(8,128)S(1)}) all-reduce(f32[32,32]{0,1:T(8,128)S(1)} %convolution_bitcast_fusion.1, f32[32,32]{0,1:T(8,128)S(1)} %convolution_bitcast_fusion), channel_id=1, replica_groups=mesh['member'=16,'dp'=32] {'member','dp'}, use_global_device_ids=true, to_apply=%region_6.10 | all-reduce | flops 2048 | bytes 16384 | tf_op jit(solution)/shard_map/psum | solution.py:78
  494.1 2.9 cholesky.55
  498.4 2.4 custom-call.13
  501.3 1.1 convolution_add_fusion.1
  (56 shorter events, 8.5 us)
Async XLA Ops:
  7.2 101.6 %copy-start = (bf16[256,64]{0,1:T(8,128)(2,1)S(1)}, bf16[256,64]{0,1:T(8,128)(2,1)}, u32[]{:S(2)}) copy-start(bf16[256,64]{0,1:T(8,128)(2,1)} %param.12) | copy-start | bytes 98308
  7.2 96.2 %all-gather.7.cloned.1.call-start = ((), (), s32[]{:S(2)}) async-start(), calls=%async_computation.2 | async-start | bytes 2179584 | tf_op jit(solution)/shard_map/all_gather | solution.py:43
  10.3 156.0 %all-gather.9.cloned.1.call-start = ((), (), s32[]{:S(2)}) async-start(), calls=%async_computation.3 | async-start | bytes 2263040 | tf_op jit(solution)/shard_map/all_gather | solution.py:62
  107.1 1.7 copy-start.4
  108.8 9.9 %copy-start.2 = (bf16[2,32,4,256]{3,2,1,0:T(4,128)(2,1)S(1)}, bf16[2,32,4,256]{3,2,1,0:T(4,128)(2,1)}, u32[]{:S(2)}) copy-start(bf16[2,32,4,256]{3,2,1,0:T(4,128)(2,1)} %param.14) | copy-start | bytes 393220
  112.1 58.0 %all-to-all-start = ((f32[2,64,256]{2,0,1:T(2,128)}), f32[2,64,256]{2,0,1:T(2,128)S(1)}, u32[]{:S(2)}, u32[]{:S(2)}) async-start(f32[2,64,256]{2,0,1:T(2,128)} %copy.43), calls=%async_computation | async-start | bytes 262144 | tf_op jit(solution)/shard_map/all_to_all | solution.py:66
  118.6 251.7 %all-gather.11.cloned.1.call-start = ((), (), s32[]{:S(2)}) async-start(), calls=%async_computation.4 | async-start | bytes 2179584 | tf_op jit(solution)/shard_map/all_gather | solution.py:43
  118.7 51.4 %copy-start.3 = (f32[4,256]{1,0:T(4,128)S(1)}, f32[4,256]{1,0:T(4,128)}, u32[]{:S(2)}) copy-start(f32[4,256]{1,0:T(4,128)} %param.13) | copy-start | bytes 12292
  379.4 3.2 copy-start.1
Sparse Core Ops, SparseCore 0:
  11.4 91.9 all-gather.6
  105.5 60.8 all-gather.8
  290.0 80.3 all-gather.10
where the time goes:
time: 512 us; the launch traced here: 511 us
  waiting for transfers between devices  219 us (43%)
  blocking collectives  217 us (42%)
  local copies, waits for them, and re-layouts  21.8 us (4%)
  other arithmetic  19.5 us (4%)
  between operations  14 us (3%)
  matrix products  13.7 us (3%)
  starting transfers between devices  6.69 us (1%)
    psum x2, blocking collectives, on_device(): gram, cross = lax.psum((gram_part, cross_part), ('member', 'dp'))  203 us
    all_gather x2, waiting for transfers between devices, predict(): gathered = lax.all_gather(rounded, 'dp', axis=0, tiled=False)  171 us
    all_gather x1, waiting for transfers between devices, on_device(): whole = lax.all_gather(own, 'member', axis=0, tiled=True)  47.6 us
    all_to_all x1, blocking collectives, on_device(): lax.all_to_all(predicted, 'member', split_axis=1, concat_axis=0, tiled=True)  13.8 us
  transfers between devices with their start and end apart: 4, of which 3 were waited for; matrix products, arithmetic and copies ran while one was open for 3% of the time, Pallas kernels for 0%

commit v1 on v0

--- a/solution.py
+++ b/solution.py
@@ -1,3 +1,4 @@
+import functools
 import jax
 import jax.numpy as jnp
 from jax import lax
@@ -5,6 +6,14 @@
 
 UPDATES = 2
 ridge_level = 0.5
+
+
+def bind_pairs_all_by_axis(local, ax_name, device_axis):
+    now = jax.lax.psum(jax.lax.psum(local, ax_name), device_axis)
+    return now
+
+
+rest_case = functools.partial(bind_pairs_all_by_axis, ax_name="dp", device_axis="member")
 
 
 def solve_gain(gram, cross):
@@ -75,7 +84,7 @@
         cross_part = lax.dot_general(
             anomaly, misfit, (((1,), (1,)), ((), ())), precision=lax.Precision.HIGHEST
         )
-        gram, cross = lax.psum((gram_part, cross_part), ("member", "dp"))
+        gram, cross = rest_case((gram_part, cross_part))
         gain = solve_gain(gram / count, cross / count)
         if update + 1 < UPDATES:
             moved = lax.dot_general(

time: 512 us -> 701 us (1.37)
  the two profiles are of different devices: /device:TPU:1 before, /device:TPU:2 now
where the time goes in v1:
time: 701 us
  blocking collectives  398 us (57%)
  waiting for transfers between devices  225 us (32%)
  local copies, waits for them, and re-layouts  21.9 us (3%)
  other arithmetic  19.6 us (3%)
  between operations  14 us (2%)
  matrix products  13.7 us (2%)
  starting transfers between devices  8.33 us (1%)
    psum x4, blocking collectives, bind_pairs_all_by_axis(): now = jax.lax.psum(jax.lax.psum(local, ax_name), device_axis)  382 us
    all_gather x2, waiting for transfers between devices, predict(): gathered = lax.all_gather(rounded, 'dp', axis=0, tiled=False)  168 us
    all_gather x1, waiting for transfers between devices, on_device(): whole = lax.all_gather(own, 'member', axis=0, tiled=True)  57 us
    all_to_all x1, blocking collectives, on_device(): lax.all_to_all(predicted, 'member', split_axis=1, concat_axis=0, tiled=True)  15.9 us
  transfers between devices with their start and end apart: 4, of which 3 were waited for; matrix products, arithmetic and copies ran while one was open for 2% of the time, Pallas kernels for 0%

profile of v1, /device:TPU:2, one launch (start us, length us, event | category | flops | bytes accessed | tf_op | source)
XLA Modules:
  0.0 700.7 jit_solution(353811854179499886)
XLA Ops:
  7.9 0.8 convert.20
  8.8 0.8 convert.19
  10.4 1.0 copy_bitcast_fusion.2
  11.4 1.4 maximum_bitcast_fusion
  12.8 88.4 %all-gather.7.cloned.1.call-done = bf16[32,2,16512]{2,1,0:T(2,128)(2,1)} async-done(((bf16[1,2,16512]{2,1,0:T(2,128)(2,1)}), bf16[32,2,16512]{2,1,0:T(2,128)(2,1)}) %all-gather.7.cloned.1.call-update) | async-done | bytes 2113552 | tf_op jit(solution)/shard_map/all_gather | solution.py:52
  101.2 0.7 convert_bitcast_fusion.1
  102.0 2.9 fusion.60
  104.9 0.8 reshape.148
  105.7 0.8 reshape.147
  106.6 2.5 fusion.20
  109.1 0.8 copy.43
  109.9 8.2 %all-to-all-start = ((f32[2,64,256]{2,0,1:T(2,128)}), f32[2,64,256]{2,0,1:T(2,128)S(1)}, u32[]{:S(2)}, u32[]{:S(2)}) async-start(f32[2,64,256]{2,0,1:T(2,128)} %copy.43), calls=%async_computation | async-start | bytes 262144 | tf_op jit(solution)/shard_map/all_to_all | solution.py:75
  118.2 57.0 %all-gather.9.cloned.1.call-done = f32[16,2,16576]{2,1,0:T(2,128)} async-done(((f32[1,2,16576]{2,1,0:T(2,128)}), f32[16,2,16576]{2,1,0:T(2,128)}) %all-gather.9.cloned.1.call-update) | async-done | bytes 2121744 | tf_op jit(solution)/shard_map/all_gather | solution.py:71
  175.3 3.7 reshape.128
  179.6 128.5 %all-reduce.1 = (f32[32,32]{0,1:T(8,128)S(1)}, f32[32,32]{0,1:T(8,128)S(1)}) all-reduce(f32[32,32]{0,1:T(8,128)S(1)} %convolution_bitcast_fusion.3, f32[32,32]{0,1:T(8,128)S(1)} %convolution_bitcast_fusion.2), channel_id=1, replica_groups=mesh['member'=16,'dp'=32] {'dp'}, use_global_device_ids=true, to_apply=%region_1.0 | all-reduce | flops 2048 | bytes 16384 | tf_op jit(solution)/shard_map/psum | solution.py:12
  308.1 61.9 %all-reduce.3 = (f32[32,32]{0,1:T(8,128)S(1)}, f32[32,32]{0,1:T(8,128)S(1)}) all-reduce(f32[32,32]{0,1:T(8,128)S(1)} %get-tuple-element.9, f32[32,32]{0,1:T(8,128)S(1)} %get-tuple-element.10), channel_id=1, replica_groups=mesh['member'=16,'dp'=32] {'member'}, use_global_device_ids=true, to_apply=%region_2.0 | all-reduce | flops 2048 | bytes 16384 | tf_op jit(solution)/shard_map/psum | solution.py:12
  370.1 2.9 cholesky.44
  374.3 2.4 custom-call.11
  377.1 4.2 convolution_add_fusion
  382.1 79.7 %all-gather.11.cloned.1.call-done = bf16[32,2,16512]{2,1,0:T(2,128)(2,1)} async-done(((bf16[1,2,16512]{2,1,0:T(2,128)(2,1)}), bf16[32,2,16512]{2,1,0:T(2,128)(2,1)}) %all-gather.11.cloned.1.call-update) | async-done | bytes 2113552 | tf_op jit(solution)/shard_map/all_gather | solution.py:52
  461.8 4.1 fusion.59
  465.8 2.6 reshape.116
  468.5 0.7 convert_bitcast_fusion
  469.2 1.6 reshape.149
  470.9 3.2 fusion.1
  474.1 0.8 fusion.17
  475.1 15.9 %all_to_all.30 = f32[2,64,256]{2,0,1:T(2,128)S(1)} all-to-all(f32[2,64,256]{2,0,1:T(2,128)S(1)} %copy.55), channel_id=1, replica_groups=mesh['member'=16,'dp'=32] {'member'}, dimensions={1} | all-to-all | bytes 262144 | tf_op jit(solution)/shard_map/all_to_all | solution.py:75
  491.6 129.1 %all-reduce = (f32[32,32]{0,1:T(8,128)S(1)}, f32[32,32]{0,1:T(8,128)S(1)}) all-reduce(f32[32,32]{0,1:T(8,128)S(1)} %convolution_bitcast_fusion.1, f32[32,32]{0,1:T(8,128)S(1)} %convolution_bitcast_fusion), channel_id=1, replica_groups=mesh['member'=16,'dp'=32] {'dp'}, use_global_device_ids=true, to_apply=%region_8.12 | all-reduce | flops 2048 | bytes 16384 | tf_op jit(solution)/shard_map/psum | solution.py:12
  620.7 62.7 %all-reduce.2 = (f32[32,32]{0,1:T(8,128)S(1)}, f32[32,32]{0,1:T(8,128)S(1)}) all-reduce(f32[32,32]{0,1:T(8,128)S(1)} %get-tuple-element.7, f32[32,32]{0,1:T(8,128)S(1)} %get-tuple-element.8), channel_id=1, replica_groups=mesh['member'=16,'dp'=32] {'member'}, use_global_device_ids=true, to_apply=%region_9.13 | all-reduce | flops 2048 | bytes 16384 | tf_op jit(solution)/shard_map/psum | solution.py:12
  683.5 2.9 cholesky.55
  687.7 2.4 custom-call.13
  690.6 1.1 convolution_add_fusion.1
  (58 shorter events, 9.9 us)
Async XLA Ops:
  7.2 99.4 %copy-start = (bf16[256,64]{0,1:T(8,128)(2,1)S(1)}, bf16[256,64]{0,1:T(8,128)(2,1)}, u32[]{:S(2)}) copy-start(bf16[256,64]{0,1:T(8,128)(2,1)} %param.12) | copy-start | bytes 98308
  7.2 94.0 %all-gather.7.cloned.1.call-start = ((), (), s32[]{:S(2)}) async-start(), calls=%async_computation.2 | async-start | bytes 2179584 | tf_op jit(solution)/shard_map/all_gather | solution.py:52
  10.3 164.9 %all-gather.9.cloned.1.call-start = ((), (), s32[]{:S(2)}) async-start(), calls=%async_computation.3 | async-start | bytes 2263040 | tf_op jit(solution)/shard_map/all_gather | solution.py:71
  104.9 1.7 copy-start.4
  106.6 11.6 %copy-start.2 = (bf16[2,32,4,256]{3,2,1,0:T(4,128)(2,1)S(1)}, bf16[2,32,4,256]{3,2,1,0:T(4,128)(2,1)}, u32[]{:S(2)}) copy-start(bf16[2,32,4,256]{3,2,1,0:T(4,128)(2,1)} %param.14) | copy-start | bytes 393220
  109.9 69.1 %all-to-all-start = ((f32[2,64,256]{2,0,1:T(2,128)}), f32[2,64,256]{2,0,1:T(2,128)S(1)}, u32[]{:S(2)}, u32[]{:S(2)}) async-start(f32[2,64,256]{2,0,1:T(2,128)} %copy.43), calls=%async_computation | async-start | bytes 262144 | tf_op jit(solution)/shard_map/all_to_all | solution.py:75
  118.1 343.7 %all-gather.11.cloned.1.call-start = ((), (), s32[]{:S(2)}) async-start(), calls=%async_computation.4 | async-start | bytes 2179584 | tf_op jit(solution)/shard_map/all_gather | solution.py:52
  118.2 60.8 %copy-start.3 = (f32[4,256]{1,0:T(4,128)S(1)}, f32[4,256]{1,0:T(4,128)}, u32[]{:S(2)}) copy-start(f32[4,256]{1,0:T(4,128)} %param.13) | copy-start | bytes 12292
  470.9 3.2 copy-start.1
Sparse Core Ops, SparseCore 0:
  11.4 89.7 all-gather.6
  103.3 71.9 all-gather.8
  382.2 79.5 all-gather.10
